TPU v7x, 32 devices: a whole 2x2x4 slice. The times are simulated.
32 devices in a mesh: grp: 2 (over y), wide: 4 (over z), col: 2 (over x), inc: 2 (over core).
Axes of the slice: x: 2, y: 2, z: 4, core: 2. Of those that a mesh axis runs over, the one named last changes fastest.
Arguments:
- values_in: bfloat16 [32, 64, 256, 512], P(('grp', 'col'), 'inc', 'wide'), parts along dimension 0, may hold values from -6 to 6
- shock_load: float32 [32], P(('grp', 'col')), parts along dimension 0, may hold values from -4 to 4
- price_field: float32 [128, 256, 512], P(('grp', 'inc'), 'wide'), parts along dimension 0, may hold values from -6 to 6
- rate_liquid: float32 [128, 256, 512], P(('grp', 'inc'), 'wide'), parts along dimension 0, may hold values from 0.05 to 0.5
- rate_illiquid: float32 [128, 256, 512], P(('grp', 'inc'), 'wide'), parts along dimension 0, may hold values from 0.05 to 0.5
- mask_liquid: int32 [128, 256, 512], P(('grp', 'inc'), 'wide'), parts along dimension 0, may hold values 0 or 1
- mask_illiquid: int32 [128, 256, 512], P(('grp', 'inc'), 'wide'), parts along dimension 0, may hold values 0 or 1
- jump_inverse: float32 [128, 64], P('grp'), parts along dimension 0, may hold values from -0.07 to 0.87
- coef_liquid: int32 [4096], replicated, may hold values from 0 to 127, as said below
- coef_illiquid: int32 [4096], replicated, may hold values from 0 to 255
- coef_income: int32 [4096], replicated, may hold values from 0 to 63
- owner: int32 [4096], replicated, may hold values from 0 to 7, as said below
Outputs:
- reduced: float32 [32, 8192], P(('grp', 'col'), ('wide', 'inc')), parts along dimension 0
There are 2 independent parts, one for each index of `grp`. A program takes and returns all parts, laid end to end along the dimension named above; an argument that names none is the same for every part. Nothing has to cross between parts.
Inputs may be any that keep to these rules, and one draw needn't show every extreme that they name: `coef_liquid`: every retained coefficient has liquid frequency below 128. No owner has more than 1024 rows, and some owner has exactly 1024.
All inputs are finite; a program needn't handle non-finite values. No bound on the sum of `mask_liquid` or of `mask_illiquid` on one device may be relied on, other than what follows from the above.
Results may differ from a plain program's by a relative error of at most 0.0003.
Values may be sent and summed in bfloat16 or wider, within the bound.
No kernel may reach another device: no remote copies, remote signals or barrier semaphores. Data moves between devices by JAX's collectives and lax.ppermute only.
A program may use at most 256 MiB of HBM per device.

v0:
```python
import jax
import jax.numpy as jnp
from jax import lax
from jax.sharding import PartitionSpec as P

NB = 512
NA = 256
NZ = 64
KBLOW = 128


def padded_2(cells, sides, width):
    for axis, dim in sides:
        count = lax.axis_size(axis)
        ends = count - 1
        head = lax.slice_in_dim(cells, 0, width, axis=dim)
        tail = lax.slice_in_dim(cells, cells.shape[dim] - width, cells.shape[dim], axis=dim)
        cells = jnp.concatenate(
            [
                lax.ppermute(tail, axis, [(i, (i + 1) % count) for i in range(ends)]),
                cells,
                lax.ppermute(head, axis, [((i + 1) % count, i) for i in range(ends)]),
            ],
            axis=dim,
        )
    return cells


def cosine_table(count):
    freq = jnp.arange(count, dtype=jnp.int32)[:, None]
    cell = jnp.arange(count, dtype=jnp.int32)[None, :]
    phase = (2 * cell + 1) * freq % (4 * count)
    angle = jnp.pi * phase.astype(jnp.float32) / (2.0 * count)
    first = jnp.where(freq == 0, jnp.sqrt(jnp.float32(0.5)), jnp.float32(1.0))
    return jnp.cos(angle) * jnp.sqrt(jnp.float32(2.0 / count)) * first


def slot_targets(owner, owners, capacity):
    onehot = (owner[:, None] == jnp.arange(owners, dtype=jnp.int32)[None, :]).astype(jnp.int32)
    before = jnp.cumsum(onehot, axis=0) - onehot
    slot = jnp.sum(before * onehot, axis=1)
    return owner * capacity + slot


def body(
    values_in,
    shock_load,
    price_field,
    rate_liquid,
    rate_illiquid,
    mask_liquid,
    mask_illiquid,
    jump_inverse,
    coef_liquid,
    coef_illiquid,
    coef_income,
    owner,
):
    high = lax.Precision.HIGHEST
    columns = values_in.shape[0]
    wide_pos = lax.axis_index("wide")
    wide_count = lax.axis_size("wide")
    padded = padded_2(values_in, (("wide", 2),), 1).astype(jnp.float32)
    center = padded[:, :, 1:-1]
    lower = jnp.where(wide_pos == 0, center[:, :, 0:1], padded[:, :, 0:1])
    upper = jnp.where(wide_pos == wide_count - 1, center[:, :, -1:], padded[:, :, -1:])
    fwd_a = jnp.concatenate([center[:, :, 1:], upper], axis=2) - center
    bwd_a = center - jnp.concatenate([lower, center[:, :, :-1]], axis=2)
    step_b = center[:, :, :, 1:] - center[:, :, :, :-1]
    zero_b = jnp.zeros(center.shape[:3] + (1,), jnp.float32)
    fwd_b = jnp.concatenate([step_b, zero_b], axis=3)
    bwd_b = jnp.concatenate([zero_b, step_b], axis=3)
    mask_b = mask_liquid.astype(jnp.float32)
    mask_a = mask_illiquid.astype(jnp.float32)
    load = shock_load[:, None, None, None]
    explicit = (
        center
        + rate_liquid * (mask_b * fwd_b - (1.0 - mask_b) * bwd_b)
        + rate_illiquid * (mask_a * fwd_a - (1.0 - mask_a) * bwd_a)
        + load * price_field
    )
    freq_rows = KBLOW
    table_b = cosine_table(NB)[:freq_rows]
    liquid_part = jnp.einsum("kb,czab->czak", table_b, explicit, precision=high)
    table_z = cosine_table(NZ)
    table_a = cosine_table(NA)
    owners = lax.axis_size(("wide", "inc"))
    capacity = 2 * owner.shape[0] // owners
    targets = slot_targets(owner, owners, capacity)
    blocks = lax.all_to_all(
        lax.all_to_all(liquid_part, "wide", split_axis=3, concat_axis=2, tiled=True),
        "inc",
        split_axis=3,
        concat_axis=1,
        tiled=True,
    )
    folded = jnp.dot(table_z, jump_inverse, precision=high)
    income_part = jnp.einsum("yz,czak->cyak", folded, blocks, precision=high)
    spectrum = jnp.einsum("ia,cjak->cjik", table_a, income_part, precision=high)
    local_rows = spectrum.shape[3]
    start = lax.axis_index(("wide", "inc")) * local_rows
    mine = (coef_liquid >= start) & (coef_liquid < start + local_rows)
    offset = jnp.clip(coef_liquid - start, 0, local_rows - 1)
    position = (coef_income * NA + coef_illiquid) * local_rows + offset
    flat = spectrum.reshape(columns, -1)
    kept = jnp.where(mine[None, :], jnp.take(flat, position, axis=1), jnp.float32(0.0))
    placed = jnp.zeros((columns, owners * capacity), jnp.float32).at[:, targets].set(kept)
    return lax.psum_scatter(placed, ("wide", "inc"), scatter_dimension=1, tiled=True)


def solution(mesh):
    placed = (
        P(("grp", "col"), "inc", "wide", None),
        P(("grp", "col")),
        P(("grp", "inc"), "wide", None),
        P(("grp", "inc"), "wide", None),
        P(("grp", "inc"), "wide", None),
        P(("grp", "inc"), "wide", None),
        P(("grp", "inc"), "wide", None),
        P("grp", None),
        P(),
        P(),
        P(),
        P(),
    )
    return jax.shard_map(
        body,
        mesh=mesh,
        in_specs=placed,
        out_specs=P(("grp", "col"), ("wide", "inc")),
        check_vma=False,
    )
```

profile of v0, /device:TPU:0, one launch (start us, length us, event | category | flops | bytes accessed | tf_op | source)
XLA Modules:
  0.0 726.5 jit_solution(2988138333981204830)
XLA Ops:
  6.5 0.0 copy-start
  6.5 3.4 fusion.115
  10.0 4.9 collective-permute-start
  15.0 1.3 collective-permute-start.1
  16.3 4.9 convert_element_type.28
  21.3 8.5 %broadcast_subtract_fusion = (f32[32,64,512]{2,1,0:T(8,128)}, f32[32,64,512]{2,1,0:T(8,128)}) fusion(s32[32,64,512]{2,1,0:T(8,128)} %param.18, s32[32,64,512]{2,1,0:T(8,128)} %param.17), kind=kLoop, calls=%fused_computation.43 | loop fusion | flops 4194304 | bytes 16777216 | tf_op jit(solution)/shard_map/sub | solution.py:79
  29.8 0.0 copy-done.2
  29.8 2.5 convert_element_type.29
  32.3 0.3 negate_select_fusion
  32.6 0.5 broadcast_compare_fusion.1
  33.1 0.0 collective-permute-done
  33.1 0.4 copy.22
  33.6 0.0 collective-permute-done.1
  33.6 0.4 copy.23
  34.0 21.0 %maximum_convert_fusion = f32[8,32,66,512]{3,2,1,0:T(8,128)} fusion(bf16[8,32,1,512]{3,2,1,0:T(2,128)(2,1)S(1)} %copy.23, bf16[8,32,64,512]{3,2,1,0:T(8,128)(2,1)} %param.12, bf16[8,32,1,512]{3,2,1,0:T(2,128)(2,1)S(1)} %copy.22), kind=kLoop, calls=%fused_computation.25 | loop fusion | flops 51904512 | bytes 51904512 | tf_op jit(solution)/shard_map/convert_element_type | solution.py:63
  55.0 0.0 copy-done.8
  55.0 47.7 %fusion.114 = (f32[8,32,63,512]{3,2,1,0:T(8,128)}, f32[8,32,63,512]{3,2,1,0:T(8,128)}) fusion(f32[8,32,66,512]{3,2,1,0:T(8,128)} %maximum_convert_fusion), kind=kLoop, calls=%fused_computation.141 | loop fusion | bytes 132120576 | tf_op jit(solution)/shard_map/slice | solution.py:68
  102.7 36.6 %slice_subtract_fusion = f32[8,32,64,511]{3,2,1,0:T(8,128)} fusion(f32[8,32,66,512]{3,2,1,0:T(8,128)} %maximum_convert_fusion), kind=kLoop, calls=%fused_computation.2 | loop fusion | flops 8372224 | bytes 100466688 | tf_op jit(solution)/shard_map/sub | solution.py:69
  139.4 0.0 slice-start
  139.4 4.9 broadcast_select_fusion
  144.2 0.0 copy-done.1
  144.3 0.0 copy-done.5
  144.3 74.5 %fusion.5 = f32[8,32,64,128]{3,2,1,0:T(8,128)} fusion(f32[8,32,1,512]{3,2,1,0:T(1,128)S(1)} %get-tuple-element.10, f32[8,32,63,512]{3,2,1,0:T(8,128)} %get-tuple-element.8, f32[8,32,63,512]{3,2,1,0:T(8,128)} %get-tuple-element.7, f32[8,32,1,512]{3,2,1,0:T(1,128)S(1)} %get-tuple-element.9, f32[8,32,66,512]{3,2,1,0:T(8,128)} %maximum_convert_fusion, ...), kind=kOutput, calls=%fused_computation.9 | convolution fusion | flops 13019512832 | bytes 173409280 | tf_op jit(solution)/shard_map/kb,czab->czak/dot_general | solution.py:84
  218.8 16.7 %copy.24 = f32[8,32,64,128]{2,1,0,3:T(8,128)} copy(f32[8,32,64,128]{3,2,1,0:T(8,128)} %fusion.5) | data formatting | bytes 16777216 | tf_op jit(solution)/shard_map/kb,czab->czak/dot_general | solution.py:84
  235.5 14.4 %reshape.110 = f32[4,1,524288]{2,1,0:T(1,128)} reshape(f32[128,8,32,64]{3,2,1,0:T(8,128)} %bitcast.55) | data formatting | bytes 16777216
  249.9 5.9 all-to-all-start
  255.9 2.3 reduce-window.6
  258.2 0.3 slice_reduce_fusion
  258.5 0.2 reduce-window.9
  258.7 0.0 copy-done
  258.7 0.3 convolution_bitcast_fusion
  259.0 0.1 add_bitcast_fusion
  259.1 0.1 fusion.71
  259.3 180.0 %all-to-all-done = f32[4,1,524288]{2,1,0:T(1,128)} async-done(((f32[4,1,524288]{2,1,0:T(1,128)}), f32[4,1,524288]{2,1,0:T(1,128)}, u32[]{:S(2)}, u32[]{:S(2)}) %all-to-all-start) | async-done | bytes 8388640 | tf_op jit(solution)/shard_map/all_to_all | solution.py:91
  439.4 0.5 broadcast.191
  439.9 28.4 %reduce.2 = f32[4,524288]{1,0:T(4,128)} reduce(f32[4,1,524288]{2,1,0:T(1,128)} %all-to-all-done, f32[]{:T(128)} %broadcast.191), dimensions={1}, to_apply=%all_to_all.26.reduce_sub_computation | reduce | bytes 16777220 | tf_op jit(solution)/shard_map/all_to_all | solution.py:91
  468.3 16.8 %reshape.111 = f32[128,8,32,64]{3,2,1,0:T(8,128)} reshape(f32[4,524288]{1,0:T(4,128)} %reduce.2) | data formatting | bytes 16777216
  485.0 21.0 %copy.39 = f32[8,32,4,64,32]{3,2,1,0,4:T(4,128)} copy(f32[8,32,4,64,32]{3,1,0,4,2:T(8,128)} %bitcast.56) | data formatting | bytes 16777216 | tf_op jit(solution)/shard_map/all_to_all | solution.py:91
  506.0 15.9 %reshape.98 = f32[8,32,256,32]{2,1,0,3:T(8,128)} reshape(f32[8,32,4,64,32]{3,2,1,0,4:T(4,128)} %copy.39) | data formatting | bytes 16777216 | tf_op jit(solution)/shard_map/all_to_all | solution.py:91
  521.9 12.1 %all_to_all.36 = f32[8,32,256,32]{2,1,0,3:T(8,128)S(1)} all-to-all(f32[8,32,256,32]{2,1,0,3:T(8,128)} %reshape.98), channel_id=1, replica_groups=mesh['grp'=2,'wide'=4,'col'=2,'inc'=2] {'inc'}, dimensions={3} | all-to-all | bytes 16777216 | tf_op jit(solution)/shard_map/all_to_all | solution.py:90
  534.0 6.7 copy.29
  540.6 13.7 %fusion.37 = f32[8,64,256,16]{2,1,3,0:T(8,128)S(1)} fusion(f32[64,64,1,1]{1,0,3,2:T(8,128)S(1)} %convolution_bitcast_fusion, f32[8,64,256,16]{2,3,1,0:T(8,128)S(1)} %bitcast.57), kind=kOutput, calls=%fused_computation.39 | convolution fusion | flops 1610612736 | bytes 16793600 | tf_op jit(solution)/shard_map/yz,czak->cyak/dot_general | solution.py:98
  554.4 13.7 %fusion.34 = f32[8,64,256,16]{2,3,1,0:T(8,128)} fusion(f32[8,64,256,16]{2,1,3,0:T(8,128)S(1)} %fusion.37, f32[256]{0:T(256)S(1)} %fusion.99, s32[256]{0:T(256)S(1)} %multiply_add_fusion.1), kind=kOutput, calls=%fused_computation.38 | convolution fusion | flops 6443433984 | bytes 16779264 | tf_op jit(solution)/shard_map/ia,cjak->cjik/dot_general | solution.py:99
  568.1 61.8 %copy.41 = f32[8,64,256,16]{0,3,2,1:T(8,128)} copy(f32[8,64,256,16]{2,3,1,0:T(8,128)} %fusion.34) | data formatting | bytes 16777216 | tf_op jit(solution)/shard_map/reshape | solution.py:105
  629.9 38.5 %scatter_custom_fusion = f32[8,8192]{0,1:T(8,128)} fusion(s32[4096]{0:T(1024)S(1)} %get-tuple-element.17, f32[]{:T(128)} %constant.42.clone.1, f32[]{:T(128)} %constant.125.clone.1, pred[4096]{0:T(1024)(128)(4,1)S(1)} %compare_and_fusion.1, pred[4096]{0:T(1024)(128)(4,1)S(1)} %compare_and_fusion, f32[8,262144]{0,1:T(8,128)} %bitcast.17, ...), kind=kCustom, calls=%fused_computation.40 | custom fusion | flops 65536 | bytes 134505984 | tf_op jit(solution)/shard_map/scatter | solution.py:107
  668.4 0.0 reduce-scatter.2.cloned.1.call-update
  668.5 49.2 %reduce-scatter.2.cloned.1.call-done = f32[8,1024]{0,1:T(8,128)} async-done(((f32[8,8192]{0,1:T(8,128)}), f32[8,1024]{0,1:T(8,128)}) %reduce-scatter.2.cloned.1.call-update) | async-done | bytes 32784 | tf_op jit(solution)/shard_map/reduce_scatter | solution.py:108
  717.6 1.8 copy.34
  (26 shorter events, 0.2 us)
Async XLA Ops:
  6.5 252.2 %copy-start = (f32[64,64]{1,0:T(8,128)S(1)}, f32[64,64]{1,0:T(8,128)}, u32[]{:S(2)}) copy-start(f32[64,64]{1,0:T(8,128)} %param.19) | copy-start | bytes 49156
  6.5 23.2 %copy-start.2 = (s32[32,64,512]{2,1,0:T(8,128)S(1)}, s32[32,64,512]{2,1,0:T(8,128)}, u32[]{:S(2)}) copy-start(s32[32,64,512]{2,1,0:T(8,128)} %param.18) | copy-start | bytes 12582916
  10.0 23.1 %collective-permute-start = (bf16[8,32,1,512]{3,1,2,0:T(8,128)(2,1)S(1)}, bf16[8,32,1,512]{3,1,2,0:T(8,128)(2,1)S(1)}, u32[]{:S(2)}, u32[]{:S(2)}) collective-permute-start(bf16[8,32,1,512]{3,1,2,0:T(8,128)(2,1)S(1)} %copy.44), channel_id=1, source_target_pairs={{0,4},{4,8},{8,12},{1,5},{5,9},{9,13},{2,6},{6,10},{10,14},{3,7},{... | collective-permute-start | bytes 786440 | tf_op jit(solution)/shard_map/ppermute | solution.py:20
  15.0 18.6 %collective-permute-start.1 = (bf16[8,32,1,512]{3,1,2,0:T(8,128)(2,1)S(1)}, bf16[8,32,1,512]{3,1,2,0:T(8,128)(2,1)S(1)}, u32[]{:S(2)}, u32[]{:S(2)}) collective-permute-start(bf16[8,32,1,512]{3,1,2,0:T(8,128)(2,1)S(1)} %copy.45), channel_id=1, source_target_pairs={{4,0},{8,4},{12,8},{5,1},{9,5},{13,9},{6,2},{10,6},{14,10},{7,3},{... | collective-permute-start | bytes 786440 | tf_op jit(solution)/shard_map/ppermute | solution.py:22
  32.3 22.7 %copy-start.8 = (f32[512]{0:T(512)}, f32[512]{0:T(512)S(1)}, u32[]{:S(2)}) copy-start(f32[512]{0:T(512)S(1)} %select_multiply_fusion) | copy-start | bytes 6148
  139.4 4.9 copy-start.1
  139.4 4.9 copy-start.5
  139.4 4.9 slice-start
  235.5 20.3 %copy-start.3 = (s32[4096]{0:T(1024)S(1)}, s32[4096]{0:T(1024)}, u32[]{:S(2)}) copy-start(s32[4096]{0:T(1024)} %param.23) | copy-start | bytes 49156
  235.5 23.7 %copy-start.4 = (s32[4096]{0:T(1024)S(1)}, s32[4096]{0:T(1024)}, u32[]{:S(2)}) copy-start(s32[4096]{0:T(1024)} %param.20) | copy-start | bytes 49156
  235.5 23.8 %copy-start.6 = (s32[4096]{0:T(1024)S(1)}, s32[4096]{0:T(1024)}, u32[]{:S(2)}) copy-start(s32[4096]{0:T(1024)} %param.21) | copy-start | bytes 49156
  235.5 23.8 %copy-start.7 = (s32[4096]{0:T(1024)S(1)}, s32[4096]{0:T(1024)}, u32[]{:S(2)}) copy-start(s32[4096]{0:T(1024)} %param.22) | copy-start | bytes 49156
  249.9 189.4 %all-to-all-start = ((f32[4,1,524288]{2,1,0:T(1,128)}), f32[4,1,524288]{2,1,0:T(1,128)}, u32[]{:S(2)}, u32[]{:S(2)}) async-start(f32[4,1,524288]{2,1,0:T(1,128)} %reshape.110), calls=%async_computation | async-start | bytes 16777216 | tf_op jit(solution)/shard_map/all_to_all | solution.py:91
  255.9 461.8 %reduce-scatter.2.cloned.1.call-start = ((), (), s32[]{:S(2)}) async-start(), calls=%async_computation.3 | async-start | bytes 4718592 | tf_op jit(solution)/shard_map/reduce_scatter | solution.py:108
Sparse Core Ops, SparseCore 0:
  668.6 49.0 reduce-scatter.1
where the time goes:
time: 733 us; the launch traced here: 727 us
  waiting for transfers between devices  229 us (31%)
  local copies, waits for them, and re-layouts  208 us (28%)
  other arithmetic  149 us (20%)
  matrix products  102 us (14%)
  between operations  13.8 us (2%)
  starting transfers between devices  12.2 us (2%)
  blocking collectives  12.1 us (2%)
    all_to_all x1, waiting for transfers between devices, body(): lax.all_to_all(liquid_part, 'wide', split_axis=3, concat_axis=2, tiled=True)  180 us
    dot_general x1, matrix products, body(): liquid_part = jnp.einsum('kb,czab->czak', table_b, explicit, precision=high)  74.5 us
    reshape x1, local copies, waits for them, and re-layouts, body(): flat = spectrum.reshape(columns, -1)  61.8 us
    reduce_scatter x1, waiting for transfers between devices, body(): lax.psum_scatter(placed, ('wide', 'inc'), scatter_dimension=1, tiled=True)  49.2 us
    slice x1, local copies, waits for them, and re-layouts, body(): bwd_a = center - jnp.concatenate([lower, center[:, :, :-1]], axis=2)  47.7 us
    scatter x1, other arithmetic, body(): jnp.zeros((columns, owners * capacity), jnp.float32).at[:, targets]  38.5 us
    all_to_all x3, local copies, waits for them, and re-layouts, body(): lax.all_to_all(liquid_part, 'wide', split_axis=3, concat_axis=2, tiled=True)  37.4 us
    sub x1, other arithmetic, body(): step_b = center[:, :, :, 1:] - center[:, :, :, :-1]  36.6 us
  transfers between devices with their start and end apart: 4, of which 2 were waited for; matrix products, arithmetic and copies ran while one was open for 3% of the time, Pallas kernels for 0%

commit v1 on v0

--- a/solution.py
+++ b/solution.py
@@ -88,7 +88,12 @@
     capacity = 2 * owner.shape[0] // owners
     targets = slot_targets(owner, owners, capacity)
     blocks = lax.all_to_all(
-        lax.all_to_all(liquid_part, "wide", split_axis=3, concat_axis=2, tiled=True),
+        jnp.concatenate(
+            lax.all_to_all(
+                jnp.stack(jnp.split(liquid_part, lax.axis_size("wide"), axis=3)), "wide", 0, 0
+            ),
+            axis=2,
+        ),
         "inc",
         split_axis=3,
         concat_axis=1,

time: 733 us -> 790 us (1.078)
  local copies, waits for them, and re-layouts: 208 us -> 244 us
  other arithmetic: 149 us -> 170 us
    another operation x0 -> x2, local copies, waits for them, and re-layouts: none -> 47.9 us  [body(): jnp.stack(jnp.split(liquid_part, lax.axis_size('wide'), axis=3))]
    reshape x0 -> x3, local copies, waits for them, and re-layouts: none -> 42.1 us  [body(): jnp.concatenate(lax.all_to_all(jnp.stack(jnp.split(liquid_part, lax.axis_...]
    all_to_all x4 -> x2, local copies, waits for them, and re-layouts: 44 us -> 7.16 us  [the longest x1 6.65 us: body(): lax.all_to_all(jnp.concatenate(lax.all_to_all(jnp.stack(jnp.split(liquid_...]
    another operation x2 -> x3, other arithmetic: 2.5 us -> 23.6 us  [the longest x1 21.1 us: body(): jnp.stack(jnp.split(liquid_part, lax.axis_size('wide'), axis=3))]
    dot_general x1 -> x0, local copies, waits for them, and re-layouts: 16.7 us -> none  [body(): liquid_part = jnp.einsum('kb,czab->czak', table_b, explicit, precision=high)]
where the time goes in v1:
time: 790 us; the launch traced here: 784 us
  local copies, waits for them, and re-layouts  244 us (31%)
  waiting for transfers between devices  229 us (29%)
  other arithmetic  170 us (22%)
  matrix products  102 us (13%)
  between operations  13.9 us (2%)
  starting transfers between devices  12.2 us (2%)
  blocking collectives  12.1 us (2%)
    all_to_all x1, waiting for transfers between devices, body(): lax.all_to_all(jnp.stack(jnp.split(liquid_part, lax.axis_size('wide'), ax...  180 us
    dot_general x1, matrix products, body(): liquid_part = jnp.einsum('kb,czab->czak', table_b, explicit, precision=high)  74.4 us
    reshape x1, local copies, waits for them, and re-layouts, body(): flat = spectrum.reshape(columns, -1)  61.7 us
    reduce_scatter x1, waiting for transfers between devices, body(): lax.psum_scatter(placed, ('wide', 'inc'), scatter_dimension=1, tiled=True)  49.1 us
    another operation x2, local copies, waits for them, and re-layouts, body(): jnp.stack(jnp.split(liquid_part, lax.axis_size('wide'), axis=3))  47.9 us
    slice x1, local copies, waits for them, and re-layouts, body(): bwd_a = center - jnp.concatenate([lower, center[:, :, :-1]], axis=2)  47.7 us
    reshape x3, local copies, waits for them, and re-layouts, body(): jnp.concatenate(lax.all_to_all(jnp.stack(jnp.split(liquid_part, lax.axis_...  42.1 us
    scatter x1, other arithmetic, body(): jnp.zeros((columns, owners * capacity), jnp.float32).at[:, targets]  38.6 us
  transfers between devices with their start and end apart: 4, of which 2 were waited for; matrix products, arithmetic and copies ran while one was open for 3% of the time, Pallas kernels for 0%

profile of v1, /device:TPU:0, one launch (start us, length us, event | category | flops | bytes accessed | tf_op | source)
XLA Modules:
  0.0 783.6 jit_solution(13779511846307264830)
XLA Ops:
  6.5 0.0 copy-start
  6.5 3.4 fusion.115
  10.0 4.9 collective-permute-start
  15.0 1.3 collective-permute-start.1
  16.3 4.9 convert_element_type.28
  21.3 8.5 %broadcast_subtract_fusion = (f32[32,64,512]{2,1,0:T(8,128)}, f32[32,64,512]{2,1,0:T(8,128)}) fusion(s32[32,64,512]{2,1,0:T(8,128)} %param.18, s32[32,64,512]{2,1,0:T(8,128)} %param.17), kind=kLoop, calls=%fused_computation.48 | loop fusion | flops 4194304 | bytes 16777216 | tf_op jit(solution)/shard_map/sub | solution.py:79
  29.8 0.0 copy-done.2
  29.8 2.5 convert_element_type.29
  32.3 0.3 negate_select_fusion
  32.5 0.5 broadcast_compare_fusion.1
  33.1 0.0 collective-permute-done
  33.1 0.4 copy.21
  33.5 0.0 collective-permute-done.1
  33.5 0.4 copy.22
  34.0 21.2 %maximum_convert_fusion = f32[8,32,66,512]{3,2,1,0:T(8,128)} fusion(bf16[8,32,1,512]{3,2,1,0:T(2,128)(2,1)S(1)} %copy.22, bf16[8,32,64,512]{3,2,1,0:T(8,128)(2,1)} %param.12, bf16[8,32,1,512]{3,2,1,0:T(2,128)(2,1)S(1)} %copy.21), kind=kLoop, calls=%fused_computation.26 | loop fusion | flops 51904512 | bytes 51904512 | tf_op jit(solution)/shard_map/convert_element_type | solution.py:63
  55.2 0.0 copy-done.8
  55.2 47.7 %fusion.114 = (f32[8,32,63,512]{3,2,1,0:T(8,128)}, f32[8,32,63,512]{3,2,1,0:T(8,128)}) fusion(f32[8,32,66,512]{3,2,1,0:T(8,128)} %maximum_convert_fusion), kind=kLoop, calls=%fused_computation.146 | loop fusion | bytes 132120576 | tf_op jit(solution)/shard_map/slice | solution.py:68
  102.9 36.5 %slice_subtract_fusion = f32[8,32,64,511]{3,2,1,0:T(8,128)} fusion(f32[8,32,66,512]{3,2,1,0:T(8,128)} %maximum_convert_fusion), kind=kLoop, calls=%fused_computation.2 | loop fusion | flops 8372224 | bytes 100466688 | tf_op jit(solution)/shard_map/sub | solution.py:69
  139.4 0.0 slice-start
  139.4 4.9 broadcast_select_fusion
  144.3 74.4 %fusion.5 = f32[8,32,64,128]{3,2,1,0:T(8,128)} fusion(f32[8,32,1,512]{3,2,1,0:T(1,128)S(1)} %get-tuple-element.10, f32[8,32,63,512]{3,2,1,0:T(8,128)} %get-tuple-element.8, f32[8,32,63,512]{3,2,1,0:T(8,128)} %get-tuple-element.7, f32[8,32,1,512]{3,2,1,0:T(1,128)S(1)} %get-tuple-element.9, f32[8,32,66,512]{3,2,1,0:T(8,128)} %maximum_convert_fusion, ...), kind=kOutput, calls=%fused_computation.9 | convolution fusion | flops 13019512832 | bytes 173409280 | tf_op jit(solution)/shard_map/kb,czab->czak/dot_general | solution.py:84
  218.7 23.3 %slice_bitcast_fusion.3 = (f32[1,8,32,64,32]{4,3,2,1,0:T(8,128)S(1)}, f32[1,8,32,64,32]{4,3,2,1,0:T(8,128)}, f32[1,8,32,64,32]{4,3,2,1,0:T(8,128)}, f32[1,8,32,64,32]{4,3,2,1,0:T(8,128)}) fusion(f32[8,32,64,128]{3,2,1,0:T(8,128)} %fusion.5), kind=kLoop, calls=%fused_computation.38 | loop fusion | bytes 16777216 | tf_op jit(solution)/shard_map/stack | solution.py:93
  242.1 21.1 %pad_maximum_fusion = f32[4,8,32,64,32]{4,3,2,1,0:T(8,128)} fusion(f32[1,8,32,64,32]{4,3,2,1,0:T(8,128)} %get-tuple-element.14, f32[1,8,32,64,32]{4,3,2,1,0:T(8,128)} %get-tuple-element.15, f32[1,8,32,64,32]{4,3,2,1,0:T(8,128)} %get-tuple-element.16, f32[1,8,32,64,32]{4,3,2,1,0:T(8,128)S(1)} %get-tuple-element.13), kind=kLoop, calls=%fused_computation.16 | loop fusion | flops 6291456 | bytes 16777216 | tf_op jit(solution)/shard_map/stack | solution.py:93
  263.1 24.6 %copy.23 = f32[4,8,32,64,32]{3,4,2,1,0:T(8,128)} copy(f32[4,8,32,64,32]{4,3,2,1,0:T(8,128)} %pad_maximum_fusion) | data formatting | bytes 16777216 | tf_op jit(solution)/shard_map/stack | solution.py:93
  287.7 14.4 %reshape.118 = f32[4,1,524288]{2,1,0:T(1,128)} reshape(f32[4,8,32,32,64]{4,3,2,1,0:T(8,128)} %bitcast.63) | data formatting | bytes 16777216
  302.1 5.9 all-to-all-start
  308.0 2.3 reduce-window.6
  310.3 0.3 slice_reduce_fusion
  310.6 0.2 reduce-window.9
  310.9 0.3 convolution_bitcast_fusion
  311.2 0.1 add_bitcast_fusion
  311.3 0.1 fusion.71
  311.5 180.0 %all-to-all-done = f32[4,1,524288]{2,1,0:T(1,128)} async-done(((f32[4,1,524288]{2,1,0:T(1,128)}), f32[4,1,524288]{2,1,0:T(1,128)}, u32[]{:S(2)}, u32[]{:S(2)}) %all-to-all-start) | async-done | bytes 8388640 | tf_op jit(solution)/shard_map/all_to_all | solution.py:92
  491.5 0.5 broadcast.191
  492.0 28.4 %reduce.2 = f32[4,524288]{1,0:T(4,128)} reduce(f32[4,1,524288]{2,1,0:T(1,128)} %all-to-all-done, f32[]{:T(128)} %broadcast.191), dimensions={1}, to_apply=%all_to_all.16.reduce_sub_computation | reduce | bytes 16777220 | tf_op jit(solution)/shard_map/all_to_all | solution.py:92
  520.5 16.8 %reshape.119 = f32[4,8,32,32,64]{4,3,2,1,0:T(8,128)} reshape(f32[4,524288]{1,0:T(4,128)} %reduce.2) | data formatting | bytes 16777216
  537.2 7.4 bitcast_bitcast_fusion.1
  544.6 18.7 %copy.36 = f32[8,32,4,64,32]{3,2,1,0,4:T(4,128)} copy(f32[8,32,4,64,32]{3,4,1,0,2:T(8,128)S(1)} %bitcast_bitcast_fusion.1) | data formatting | bytes 16777216 | tf_op jit(solution)/shard_map/reshape | solution.py:91
  563.4 15.9 %reshape.106 = f32[8,32,256,32]{2,1,0,3:T(8,128)} reshape(f32[8,32,4,64,32]{3,2,1,0,4:T(4,128)} %copy.36) | data formatting | bytes 16777216 | tf_op jit(solution)/shard_map/reshape | solution.py:91
  579.3 12.1 %all_to_all.23 = f32[8,32,256,32]{2,1,0,3:T(8,128)S(1)} all-to-all(f32[8,32,256,32]{2,1,0,3:T(8,128)} %reshape.106), channel_id=1, replica_groups=mesh['grp'=2,'wide'=4,'col'=2,'inc'=2] {'inc'}, dimensions={3} | all-to-all | bytes 16777216 | tf_op jit(solution)/shard_map/all_to_all | solution.py:90
  591.4 6.7 copy.27
  598.0 13.5 %fusion.37 = f32[8,64,256,16]{2,1,3,0:T(8,128)S(1)} fusion(f32[64,64,1,1]{1,0,3,2:T(8,128)S(1)} %convolution_bitcast_fusion, f32[8,64,256,16]{2,3,1,0:T(8,128)S(1)} %bitcast.64), kind=kOutput, calls=%fused_computation.44 | convolution fusion | flops 1610612736 | bytes 16793600 | tf_op jit(solution)/shard_map/yz,czak->cyak/dot_general | solution.py:103
  611.5 13.8 %fusion.34 = f32[8,64,256,16]{2,3,1,0:T(8,128)} fusion(f32[8,64,256,16]{2,1,3,0:T(8,128)S(1)} %fusion.37, f32[256]{0:T(256)S(1)} %fusion.99, s32[256]{0:T(256)S(1)} %multiply_add_fusion.1), kind=kOutput, calls=%fused_computation.43 | convolution fusion | flops 6443433984 | bytes 16779264 | tf_op jit(solution)/shard_map/ia,cjak->cjik/dot_general | solution.py:104
  625.3 61.7 %copy.38 = f32[8,64,256,16]{0,3,2,1:T(8,128)} copy(f32[8,64,256,16]{2,3,1,0:T(8,128)} %fusion.34) | data formatting | bytes 16777216 | tf_op jit(solution)/shard_map/reshape | solution.py:110
  687.0 38.6 %scatter_custom_fusion = f32[8,8192]{0,1:T(8,128)} fusion(s32[4096]{0:T(1024)S(1)} %get-tuple-element.21, f32[]{:T(128)} %constant.42.clone.1, f32[]{:T(128)} %constant.125.clone.1, pred[4096]{0:T(1024)(128)(4,1)S(1)} %compare_and_fusion.1, pred[4096]{0:T(1024)(128)(4,1)S(1)} %compare_and_fusion, f32[8,262144]{0,1:T(8,128)} %bitcast.19, ...), kind=kCustom, calls=%fused_computation.45 | custom fusion | flops 65536 | bytes 134505984 | tf_op jit(solution)/shard_map/scatter | solution.py:112
  725.5 0.0 reduce-scatter.2.cloned.1.call-update
  725.6 49.1 %reduce-scatter.2.cloned.1.call-done = f32[8,1024]{0,1:T(8,128)} async-done(((f32[8,8192]{0,1:T(8,128)}), f32[8,1024]{0,1:T(8,128)}) %reduce-scatter.2.cloned.1.call-update) | async-done | bytes 32784 | tf_op jit(solution)/shard_map/reduce_scatter | solution.py:113
  774.7 1.8 copy.32
  (29 shorter events, 0.2 us)
Async XLA Ops:
  6.5 304.3 %copy-start = (f32[64,64]{1,0:T(8,128)S(1)}, f32[64,64]{1,0:T(8,128)}, u32[]{:S(2)}) copy-start(f32[64,64]{1,0:T(8,128)} %param.19) | copy-start | bytes 49156
  6.5 23.2 %copy-start.2 = (s32[32,64,512]{2,1,0:T(8,128)S(1)}, s32[32,64,512]{2,1,0:T(8,128)}, u32[]{:S(2)}) copy-start(s32[32,64,512]{2,1,0:T(8,128)} %param.18) | copy-start | bytes 12582916
  10.0 23.1 %collective-permute-start = (bf16[8,32,1,512]{3,1,2,0:T(8,128)(2,1)S(1)}, bf16[8,32,1,512]{3,1,2,0:T(8,128)(2,1)S(1)}, u32[]{:S(2)}, u32[]{:S(2)}) collective-permute-start(bf16[8,32,1,512]{3,1,2,0:T(8,128)(2,1)S(1)} %copy.41), channel_id=1, source_target_pairs={{0,4},{4,8},{8,12},{1,5},{5,9},{9,13},{2,6},{6,10},{10,14},{3,7},{... | collective-permute-start | bytes 786440 | tf_op jit(solution)/shard_map/ppermute | solution.py:20
  15.0 18.5 %collective-permute-start.1 = (bf16[8,32,1,512]{3,1,2,0:T(8,128)(2,1)S(1)}, bf16[8,32,1,512]{3,1,2,0:T(8,128)(2,1)S(1)}, u32[]{:S(2)}, u32[]{:S(2)}) collective-permute-start(bf16[8,32,1,512]{3,1,2,0:T(8,128)(2,1)S(1)} %copy.42), channel_id=1, source_target_pairs={{4,0},{8,4},{12,8},{5,1},{9,5},{13,9},{6,2},{10,6},{14,10},{7,3},{... | collective-permute-start | bytes 786440 | tf_op jit(solution)/shard_map/ppermute | solution.py:22
  32.3 22.9 %copy-start.8 = (f32[512]{0:T(512)}, f32[512]{0:T(512)S(1)}, u32[]{:S(2)}) copy-start(f32[512]{0:T(512)S(1)} %select_multiply_fusion) | copy-start | bytes 6148
  139.4 4.9 copy-start.1
  139.4 4.9 copy-start.5
  139.4 4.9 slice-start
  287.7 20.3 %copy-start.3 = (s32[4096]{0:T(1024)S(1)}, s32[4096]{0:T(1024)}, u32[]{:S(2)}) copy-start(s32[4096]{0:T(1024)} %param.23) | copy-start | bytes 49156
  287.7 23.7 %copy-start.4 = (s32[4096]{0:T(1024)S(1)}, s32[4096]{0:T(1024)}, u32[]{:S(2)}) copy-start(s32[4096]{0:T(1024)} %param.20) | copy-start | bytes 49156
  287.7 23.7 %copy-start.6 = (s32[4096]{0:T(1024)S(1)}, s32[4096]{0:T(1024)}, u32[]{:S(2)}) copy-start(s32[4096]{0:T(1024)} %param.21) | copy-start | bytes 49156
  287.7 23.8 %copy-start.7 = (s32[4096]{0:T(1024)S(1)}, s32[4096]{0:T(1024)}, u32[]{:S(2)}) copy-start(s32[4096]{0:T(1024)} %param.22) | copy-start | bytes 49156
  302.1 189.4 %all-to-all-start = ((f32[4,1,524288]{2,1,0:T(1,128)}), f32[4,1,524288]{2,1,0:T(1,128)}, u32[]{:S(2)}, u32[]{:S(2)}) async-start(f32[4,1,524288]{2,1,0:T(1,128)} %reshape.118), calls=%async_computation | async-start | bytes 16777216 | tf_op jit(solution)/shard_map/all_to_all | solution.py:92
  308.0 466.7 %reduce-scatter.2.cloned.1.call-start = ((), (), s32[]{:S(2)}) async-start(), calls=%async_computation.3 | async-start | bytes 4718592 | tf_op jit(solution)/shard_map/reduce_scatter | solution.py:113
Sparse Core Ops, SparseCore 0:
  725.7 48.9 reduce-scatter.1
